TPU v7x, 256 devices: a whole 4x4x8 slice. The times are simulated.
256 devices in a mesh: seq: 32 (over y, z), tensor: 8 (over x, core).
Axes of the slice: x: 4, y: 4, z: 8, core: 2. Of those that a mesh axis runs over, the one named last changes fastest.
Arguments:
- query: bfloat16 [4096, 2048], P('seq', 'tensor')
- suffix_kv: bfloat16 [4096, 4, 2, 128], P('seq'), may hold values from -6 to 6
- segment_ids: int32 [32, 128], P('seq'), may hold values from 0 to 3, never falling along the last dimension, each value on 1 to 64 neighbouring positions
- request_prefix: int32 [32, 4], P('seq'), may hold values from 0 to 3
- prefix_kv: bfloat16 [32768, 4, 2, 128], P('seq')
- shard_prefix: int32 [32], P('seq'), may hold values from 0 to 3, as said below
- residual: bfloat16 [4096, 2048], P('seq'), may hold values from -3.2 to 3.2
- out_weight: bfloat16 [2048, 2048], P('tensor'), may hold values from -0.1875 to 0.1875
- norm_gain: float32 [2048], replicated, may hold values from 0.1 to 1.9
- expert_ids: int32 [4096, 6], P('seq'), may hold values from 0 to 63, all different within a row; in each aligned block of 128 rows (0 to 127, 128 to 255, ...) at most 24 rows name the same one
- gate_weights: float32 [4096, 6], P('seq'), may hold values from 0.05 to 0.5
- expert_in: bfloat16 [64, 2048, 2, 1408], P('seq', None, None, 'tensor'), may hold values from -0.125 to 0.125
- expert_out: bfloat16 [64, 1408, 2048], P('seq', 'tensor'), may hold values from -0.21875 to 0.21875
Outputs:
- attended: bfloat16 [4096, 2048], P('seq', 'tensor')
- layer_out: bfloat16 [4096, 2048], P('seq', 'tensor')
Inputs may be any that keep to these rules, and one draw needn't show every extreme that they name: `segment_ids`: on each seq index the segment numbers never fall along the 128 positions and every number occurs. `shard_prefix`: every prefix owns the same number of shards. `expert_ids`: each row names 6 different experts; within the 128 rows of one seq index no expert is named more than 24 times, and that count is reached.
All inputs are finite; a program needn't handle non-finite values.
Results may differ from a plain program's by a relative error of at most 0.02.
Values may be sent and summed in bfloat16 or wider, within the bound.
No kernel may reach another device: no remote copies, remote signals or barrier semaphores. Data moves between devices by JAX's collectives and lax.ppermute only.
A program may use at most 128 MiB of HBM per device.

v0:
```python
import jax
import jax.numpy as jnp
from jax import lax
from jax.sharding import PartitionSpec as P

QH = 16
KVH = 4
NEG_FLOOR = -1e30


def fold_block(carried, queries, key_rows, values, allowed, score_scale):
    running_max, running_sum, weighted = carried
    scores = (
        jnp.einsum("rhd,kd->rhk", queries, key_rows, preferred_element_type=jnp.float32)
        * score_scale
    )
    scores = jnp.where(allowed[:, None, :], scores, -jnp.inf)
    new_max = jnp.maximum(running_max, jnp.max(scores, axis=2))
    weights = jnp.exp(scores - new_max[:, :, None])
    shrink = jnp.exp(running_max - new_max)
    gathered = jnp.einsum(
        "rhk,kd->rhd", weights.astype(jnp.bfloat16), values, preferred_element_type=jnp.float32
    )
    return (
        new_max,
        running_sum * shrink + jnp.sum(weights, axis=2),
        weighted * shrink[:, :, None] + gathered,
    )


def body(
    query,
    suffix_kv,
    segment_ids,
    request_prefix,
    prefix_kv,
    shard_prefix,
    residual,
    out_weight,
    norm_gain,
    expert_ids,
    gate_weights,
    expert_in,
    expert_out,
):
    tok_rows = query.shape[0]
    head_size = suffix_kv.shape[3]
    heads_here = query.shape[1] // head_size
    kv_head = lax.axis_index("tensor") * heads_here // (QH // KVH)
    score_scale = head_size ** (-0.5)
    queries = query.reshape(tok_rows, heads_here, head_size)
    segments = segment_ids[0]
    requests = jnp.arange(request_prefix.shape[1], dtype=jnp.int32)
    row_prefix = jnp.sum(
        jnp.where(segments[:, None] == requests[None, :], request_prefix[0][None, :], 0), axis=1
    )
    blank_state = (
        jnp.full((tok_rows, heads_here), NEG_FLOOR, jnp.float32),
        jnp.zeros((tok_rows, heads_here), jnp.float32),
        jnp.zeros((tok_rows, heads_here, head_size), jnp.float32),
    )
    shard_len = prefix_kv.shape[0]
    own_cache = lax.dynamic_slice_in_dim(prefix_kv, kv_head, 1, 1).reshape(shard_len, 2 * head_size)
    cache_rows = lax.all_gather(own_cache, "seq", axis=0, tiled=True)
    owners = lax.all_gather(shard_prefix, "seq", axis=0, tiled=True)
    shard_count = owners.shape[0]
    shards = cache_rows.reshape(shard_count, -1, 2, head_size)

    def one_shard(inner_state, shard_item):
        block_rows, shard_owner = shard_item
        matching = row_prefix == shard_owner

        def attend(current):
            allowed = jnp.broadcast_to(matching[:, None], (tok_rows, block_rows.shape[0]))
            return fold_block(
                current, queries, block_rows[:, 0], block_rows[:, 1], allowed, score_scale
            )

        return (lax.cond(jnp.any(matching), attend, lambda current: current, inner_state), None)

    final_state, unused = lax.scan(one_shard, blank_state, (shards, owners))
    carried = final_state
    own_suffix = lax.dynamic_slice_in_dim(suffix_kv, kv_head, 1, 1).reshape(tok_rows, 2, head_size)
    positions = jnp.arange(tok_rows)
    causal = (segments[:, None] == segments[None, :]) & (positions[None, :] <= positions[:, None])
    carried = fold_block(carried, queries, own_suffix[:, 0], own_suffix[:, 1], causal, score_scale)
    running_max, running_sum, weighted = carried
    attention = (
        (weighted / running_sum[:, :, None])
        .reshape(tok_rows, heads_here * head_size)
        .astype(jnp.bfloat16)
    )
    projected = jnp.dot(attention, out_weight, preferred_element_type=jnp.float32)
    model_width = residual.shape[1]
    slice_width = model_width // lax.axis_size("tensor")
    first_col = lax.axis_index("tensor") * slice_width
    shared = lax.psum_scatter(projected, "tensor", scatter_dimension=1, tiled=True)
    hidden_state = (
        lax.dynamic_slice_in_dim(residual, first_col, slice_width, 1).astype(jnp.float32) + shared
    )
    squares = lax.psum(jnp.sum(hidden_state * hidden_state, axis=1), "tensor")
    gain_cols = lax.dynamic_slice_in_dim(norm_gain, first_col, slice_width, 0)
    normed = (
        hidden_state * lax.rsqrt(squares / model_width + 1e-06)[:, None] * gain_cols[None, :]
    ).astype(jnp.bfloat16)
    attended = hidden_state.astype(jnp.bfloat16)
    exp_here = expert_in.shape[0]
    sources = lax.axis_size("seq")
    experts = exp_here * sources
    top_k = expert_ids.shape[1]
    capacity = 2 * tok_rows * top_k // experts
    flat_ids = expert_ids.reshape(-1)
    onehot = (flat_ids[:, None] == jnp.arange(experts, dtype=jnp.int32)[None, :]).astype(jnp.int32)
    slot_index = jnp.sum((jnp.cumsum(onehot, axis=0) - 1) * onehot, axis=1)
    places = flat_ids * capacity + slot_index
    outgoing = (
        jnp.zeros((experts * capacity, slice_width), jnp.bfloat16)
        .at[places]
        .set(jnp.repeat(normed, top_k, axis=0))
    )
    incoming = lax.all_to_all(
        outgoing.reshape(sources, exp_here, capacity, slice_width),
        "seq",
        split_axis=0,
        concat_axis=0,
        tiled=True,
    )
    gate_up = jnp.einsum(
        "sjcd,jdgh->sjcgh",
        lax.all_gather(incoming, "tensor", axis=3, tiled=True),
        expert_in,
        preferred_element_type=jnp.float32,
    )
    hidden = (jax.nn.silu(gate_up[:, :, :, 0]) * gate_up[:, :, :, 1]).astype(jnp.bfloat16)
    group_terms = jnp.einsum(
        "sjch,jhd->sjcd", hidden, expert_out, preferred_element_type=jnp.float32
    )
    expert_rows_out = lax.psum_scatter(
        group_terms.astype(jnp.bfloat16), "tensor", scatter_dimension=3, tiled=True
    )
    returned = lax.all_to_all(expert_rows_out, "seq", split_axis=0, concat_axis=0, tiled=True)
    picked = returned.reshape(experts * capacity, slice_width)[places].reshape(
        tok_rows, top_k, slice_width
    )
    mixture = jnp.sum(gate_weights[:, :, None] * picked.astype(jnp.float32), axis=1)
    layer_out = (hidden_state + mixture).astype(jnp.bfloat16)
    return (attended, layer_out)


def solution(mesh):
    in_specs = (
        P("seq", "tensor"),
        P("seq", None, None, None),
        P("seq", None),
        P("seq", None),
        P("seq", None, None, None),
        P("seq"),
        P("seq", None),
        P("tensor", None),
        P(),
        P("seq", None),
        P("seq", None),
        P("seq", None, None, "tensor"),
        P("seq", "tensor", None),
    )
    out_specs = (P("seq", "tensor"), P("seq", "tensor"))
    return jax.shard_map(body, mesh=mesh, in_specs=in_specs, out_specs=out_specs, check_vma=False)
```

profile of v0, /device:TPU:32, one launch (start us, length us, event | category | flops | bytes accessed | tf_op | source)
XLA Modules:
  0.0 573.5 jit_solution(9225628321920478958)
XLA Ops:
  7.3 1.6 constant_dynamic-slice_fusion.1
  14.0 23.0 %all-reduce = s32[32]{0:T(128)S(1)} all-reduce(s32[32]{0:T(128)S(1)} %dynamic-update-slice), channel_id=1, replica_groups=mesh['seq'=32,'tensor'=8] {'seq'}, use_global_device_ids=true, to_apply=%add | all-reduce | flops 32 | bytes 256
  37.4 113.8 %all-gather.3.cloned.1.call-done = bf16[32768,256]{0,1:T(8,128)(2,1)} async-done(((bf16[1024,256]{0,1:T(8,128)(2,1)}), bf16[32768,256]{0,1:T(8,128)(2,1)}) %all-gather.3.cloned.1.call-update) | async-done | bytes 16777232 | tf_op jit(solution)/shard_map/all_gather | solution.py:64
  151.2 18.7 %copy.104 = bf16[32,8,32,1024]{3,2,1,0:T(8,128)(2,1)} copy(bf16[32,8,32,1024]{3,1,2,0:T(8,128)(2,1)} %bitcast.106) | data formatting | bytes 33554432
  169.8 23.0 %copy.78 = bf16[32,1024,2,128]{3,1,2,0:T(8,128)(2,1)} copy(bf16[32,1024,2,128]{1,0,3,2:T(8,128)(2,1)} %bitcast.105) | data formatting | bytes 33554432 | tf_op jit(solution)/shard_map/while | solution.py:81
  192.9 111.5 %while.14 = (s32[]{:T(128)}, f32[128,2]{0,1:T(2,128)S(1)}, f32[128,2]{0,1:T(2,128)S(1)}, f32[128,2,128]{2,0,1:T(8,128)S(1)}, s32[32]{0:T(128)S(1)}, /*index=5*/s...) while((s32[]{:T(128)}, f32[128,2]{0,1:T(2,128)S(1)}, ...), condition=%wide.region_7.8_spmd, body=%wide.region_1.7_spmd.sunk | while | flops 136119040 | bytes 5064039 | solution.py:81
  195.3 2.0 conditional.2
  199.8 2.1 conditional.2
  204.9 1.3 fusion.45
  209.2 2.0 conditional.2
  213.7 2.1 conditional.2
  218.9 1.3 fusion.45
  221.3 1.3 fusion.45
  223.2 2.0 conditional.2
  225.8 1.3 fusion.45
  232.6 2.0 conditional.2
  237.7 1.3 fusion.45
  239.6 2.1 conditional.2
  246.5 2.0 conditional.2
  253.5 2.1 conditional.2
  256.2 1.3 fusion.45
  258.0 2.1 conditional.2
  268.1 1.3 fusion.45
  269.9 2.0 conditional.2
  272.6 1.3 fusion.45
  274.4 2.1 conditional.2
  277.1 1.3 fusion.45
  286.3 2.0 conditional.2
  291.4 1.3 fusion.45
  293.3 2.1 conditional.2
  297.8 2.1 conditional.2
  302.3 2.1 conditional.2
  304.8 2.6 fusion.39
  307.8 1.8 reduce-window.6
  311.1 59.8 %reduce-scatter.3.cloned.1.call-done = f32[128,256]{1,0:T(8,128)} async-done(((f32[128,2048]{1,0:T(8,128)}), f32[128,256]{1,0:T(8,128)}) %reduce-scatter.3.cloned.1.call-update) | async-done | bytes 131088 | tf_op jit(solution)/shard_map/reduce_scatter | solution.py:97
  371.9 12.9 %psum.7 = f32[128]{0:T(128)S(1)} all-reduce(f32[128]{0:T(128)S(1)} %multiply_reduce_fusion.1), channel_id=1, replica_groups=mesh['seq'=32,'tensor'=8] {'tensor'}, use_global_device_ids=true, to_apply=%region_15.16 | all-reduce | flops 128 | bytes 1024 | tf_op jit(solution)/shard_map/psum | solution.py:101
  386.8 6.7 %scatter_custom_fusion = bf16[1536,256]{1,0:T(8,128)(2,1)} fusion(s32[768]{0:T(1024)S(1)} %fusion.33, bf16[768,256]{1,0:T(8,128)(2,1)} %reshape.146, bf16[]{:T(256)} %constant.72.clone.1), kind=kCustom, calls=%fused_computation.34 | custom fusion | bytes 786944 | tf_op jit(solution)/shard_map/scatter | solution.py:119
  393.5 32.7 %all_to_all.10 = bf16[32,2,24,256]{3,2,1,0:T(8,128)(2,1)S(1)} all-to-all(bf16[32,2,24,256]{3,2,1,0:T(8,128)(2,1)} %bitcast.107), channel_id=1, replica_groups=mesh['seq'=32,'tensor'=8] {'seq'}, dimensions={0} | all-to-all | bytes 1572864 | tf_op jit(solution)/shard_map/all_to_all | solution.py:121
  427.4 40.6 %all-gather.5.cloned.1.call-done = bf16[32,2,24,2048]{3,2,0,1:T(8,128)(2,1)} async-done(((bf16[32,2,24,256]{3,2,0,1:T(8,128)(2,1)}), bf16[32,2,24,2048]{3,2,0,1:T(8,128)(2,1)}) %all-gather.5.cloned.1.call-update) | async-done | bytes 6291472 | tf_op jit(solution)/shard_map/all_gather | solution.py:130
  468.0 5.7 fusion.9
  473.7 4.6 convert_bitcast_fusion
  478.3 46.1 %reduce-scatter.5.cloned.1.call-done = bf16[32,2,24,256]{3,2,0,1:T(8,128)(2,1)} async-done(((bf16[32,2,24,2048]{3,2,0,1:T(8,128)(2,1)}), bf16[32,2,24,256]{3,2,0,1:T(8,128)(2,1)}) %reduce-scatter.5.cloned.1.call-update) | async-done | bytes 786448 | tf_op jit(solution)/shard_map/reduce_scatter | solution.py:138
  524.4 2.1 copy.92
  526.5 10.1 %all-to-all-start.1 = ((bf16[32,2,24,256]{3,2,1,0:T(8,128)(2,1)}), bf16[32,2,24,256]{3,2,1,0:T(8,128)(2,1)}, u32[]{:S(2)}, u32[]{:S(2)}) async-start(bf16[32,2,24,256]{3,2,1,0:T(8,128)(2,1)} %copy.92), calls=%async_computation.3 | async-start | bytes 1572864 | tf_op jit(solution)/shard_map/all_to_all | solution.py:141
  536.8 22.6 %all-to-all-done.1 = bf16[32,2,24,256]{3,2,1,0:T(8,128)(2,1)} async-done(((bf16[32,2,24,256]{3,2,1,0:T(8,128)(2,1)}), bf16[32,2,24,256]{3,2,1,0:T(8,128)(2,1)}, u32[]{:S(2)}, u32[]{:S(2)}) %all-to-all-start.1) | async-done | bytes 786464 | tf_op jit(solution)/shard_map/all_to_all | solution.py:141
  559.3 3.4 gather_fusion
  563.8 1.6 multiply_reduce_fusion
  565.4 1.5 add_convert_fusion
  (246 shorter events, 91.7 us)
Async XLA Ops:
  7.2 460.8 %copy-start = (bf16[2,2048,2,176]{1,3,2,0:T(8,128)(2,1)S(1)}, bf16[2,2048,2,176]{1,3,2,0:T(8,128)(2,1)}, u32[]{:S(2)}) copy-start(bf16[2,2048,2,176]{1,3,2,0:T(8,128)(2,1)} %param.28) | copy-start | bytes 8650756
  7.2 5.5 copy-start.7
  7.2 29.8 %copy-start.4 = (s32[1,128]{1,0:T(1,128)S(1)}, s32[1,128]{1,0:T(1,128)}, u32[]{:S(2)}) copy-start(s32[1,128]{1,0:T(1,128)} %param.19) | copy-start | bytes 1540
  7.2 29.8 %copy-start.6 = (s32[1,4]{1,0:T(1,128)S(1)}, s32[1,4]{1,0:T(1,128)}, u32[]{:S(2)}) copy-start(s32[1,4]{1,0:T(1,128)} %param.20) | copy-start | bytes 52
  7.2 144.0 %all-gather.3.cloned.1.call-start = ((), (), s32[]{:S(2)}) async-start(), calls=%async_computation.4 | async-start | bytes 17301504 | tf_op jit(solution)/shard_map/all_gather | solution.py:64
  10.0 360.9 %reduce-scatter.3.cloned.1.call-start = ((), (), s32[]{:S(2)}) async-start(), calls=%async_computation.5 | async-start | bytes 1179648 | tf_op jit(solution)/shard_map/reduce_scatter | solution.py:97
  304.4 3.0 copy-start.2
  307.4 160.7 %all-gather.5.cloned.1.call-start = ((), (), s32[]{:S(2)}) async-start(), calls=%async_computation.6 | async-start | bytes 7077888 | tf_op jit(solution)/shard_map/all_gather | solution.py:130
  427.2 97.2 %reduce-scatter.5.cloned.1.call-start = ((), (), s32[]{:S(2)}) async-start(), calls=%async_computation.7 | async-start | bytes 7077888 | tf_op jit(solution)/shard_map/reduce_scatter | solution.py:138
  468.0 5.7 copy-start.5
  478.3 58.4 %copy-start.3 = (f32[128,6]{0,1:T(8,128)S(1)}, f32[128,6]{0,1:T(8,128)}, u32[]{:S(2)}) copy-start(f32[128,6]{0,1:T(8,128)} %param.27) | copy-start | bytes 9220
  526.5 32.8 %all-to-all-start.1 = ((bf16[32,2,24,256]{3,2,1,0:T(8,128)(2,1)}), bf16[32,2,24,256]{3,2,1,0:T(8,128)(2,1)}, u32[]{:S(2)}, u32[]{:S(2)}) async-start(bf16[32,2,24,256]{3,2,1,0:T(8,128)(2,1)} %copy.92), calls=%async_computation.3 | async-start | bytes 1572864 | tf_op jit(solution)/shard_map/all_to_all | solution.py:141
  559.3 6.1 %copy-start.1 = (f32[128,256]{1,0:T(8,128)S(1)}, f32[128,256]{1,0:T(8,128)}, u32[]{:S(2)}) copy-start(f32[128,256]{1,0:T(8,128)} %reduce-scatter.3.cloned.1.call-done) | copy-start | bytes 393220
Sparse Core Ops, SparseCore 0:
  10.6 140.5 all-gather.2
  307.5 63.3 reduce-scatter.2
  427.3 40.6 all-gather.4
  478.4 45.9 reduce-scatter.4
where the time goes:
time: 577 us; the launch traced here: 573 us
  waiting for transfers between devices  283 us (49%)
  local copies, waits for them, and re-layouts  101 us (18%)
  blocking collectives  68.6 us (12%)
  other arithmetic  51 us (9%)
  matrix products  25 us (4%)
  loops' own time  19.9 us (3%)
  between operations  14.7 us (3%)
  starting transfers between devices  10.5 us (2%)
    all_gather x1, waiting for transfers between devices, body(): cache_rows = lax.all_gather(own_cache, 'seq', axis=0, tiled=True)  114 us
    reduce_scatter x1, waiting for transfers between devices, body(): lax.psum_scatter(projected, 'tensor', scatter_dimension=1, tiled=True)  59.8 us
    reduce_scatter x1, waiting for transfers between devices, body(): lax.psum_scatter(group_terms.astype(jnp.bfloat16), 'tensor', scatter_dime...  46.1 us
    reduce_or x32, other arithmetic, one_shard(): jnp.any(matching)  40.7 us
    all_gather x1, waiting for transfers between devices, body(): lax.all_gather(incoming, 'tensor', axis=3, tiled=True)  40.6 us
    all_to_all x1, blocking collectives, body(): lax.all_to_all(outgoing.reshape(sources, exp_here, capacity, slice_width)...  32.7 us
    while x3, local copies, waits for them, and re-layouts, body(): final_state, unused = lax.scan(one_shard, blank_state, (shards, owners))  23.2 us
    unnamed x1, blocking collectives  23 us
  transfers between devices with their start and end apart: 5, of which 5 were waited for; matrix products, arithmetic and copies ran while one was open for 1% of the time, Pallas kernels for 0%

commit v1 on v0

--- a/solution.py
+++ b/solution.py
@@ -127,7 +127,9 @@
     )
     gate_up = jnp.einsum(
         "sjcd,jdgh->sjcgh",
-        lax.all_gather(incoming, "tensor", axis=3, tiled=True),
+        jnp.concatenate(
+            lax.all_to_all(jnp.stack([incoming] * lax.axis_size("tensor")), "tensor", 0, 0), axis=3
+        ),
         expert_in,
         preferred_element_type=jnp.float32,
     )

time: 577 us -> 624 us (1.081)
  blocking collectives: 68.6 us -> 143 us
  waiting for transfers between devices: 283 us -> 236 us
  local copies, waits for them, and re-layouts: 101 us -> 121 us
    all_to_all x0 -> x1, blocking collectives: none -> 74.7 us  [body(): lax.all_to_all(jnp.stack([incoming] * lax.axis_size('tensor')), 'tensor',...]
    all_gather x1 -> x0, waiting for transfers between devices: 40.6 us -> none  [body(): lax.all_gather(incoming, 'tensor', axis=3, tiled=True)]
    reshape x0 -> x2, local copies, waits for them, and re-layouts: none -> 20.1 us  [body(): jnp.concatenate(lax.all_to_all(jnp.stack([incoming] * lax.axis_size('tens...]
    reduce_scatter x1, waiting for transfers between devices: 46.1 us -> 39.7 us  [body(): lax.psum_scatter(group_terms.astype(jnp.bfloat16), 'tensor', scatter_dime...]
  transfers between devices with their start and end apart: 5 -> 4, of which waited for: 5 -> 4; matrix products, arithmetic and copies ran while one was open for 1% -> 1% of each run, Pallas kernels for 0% -> 0%
where the time goes in v1:
time: 624 us; the launch traced here: 621 us
  waiting for transfers between devices  236 us (38%)
  blocking collectives  143 us (23%)
  local copies, waits for them, and re-layouts  121 us (19%)
  other arithmetic  51 us (8%)
  matrix products  25 us (4%)
  loops' own time  19.9 us (3%)
  between operations  14.7 us (2%)
  starting transfers between devices  10.3 us (2%)
    all_gather x1, waiting for transfers between devices, body(): cache_rows = lax.all_gather(own_cache, 'seq', axis=0, tiled=True)  114 us
    all_to_all x1, blocking collectives, body(): lax.all_to_all(jnp.stack([incoming] * lax.axis_size('tensor')), 'tensor',...  74.7 us
    reduce_scatter x1, waiting for transfers between devices, body(): lax.psum_scatter(projected, 'tensor', scatter_dimension=1, tiled=True)  59.8 us
    reduce_or x32, other arithmetic, one_shard(): jnp.any(matching)  40.7 us
    reduce_scatter x1, waiting for transfers between devices, body(): lax.psum_scatter(group_terms.astype(jnp.bfloat16), 'tensor', scatter_dime...  39.7 us
    all_to_all x1, blocking collectives, body(): lax.all_to_all(outgoing.reshape(sources, exp_here, capacity, slice_width)...  32.7 us
    while x3, local copies, waits for them, and re-layouts, body(): final_state, unused = lax.scan(one_shard, blank_state, (shards, owners))  23.2 us
    unnamed x1, blocking collectives  23 us
  transfers between devices with their start and end apart: 4, of which 4 were waited for; matrix products, arithmetic and copies ran while one was open for 1% of the time, Pallas kernels for 0%

profile of v1, /device:TPU:32, one launch (start us, length us, event | category | flops | bytes accessed | tf_op | source)
XLA Modules:
  0.0 620.7 jit_solution(17263645362288191511)
XLA Ops:
  7.3 1.6 constant_dynamic-slice_fusion.1
  14.0 23.0 %all-reduce = s32[32]{0:T(128)S(1)} all-reduce(s32[32]{0:T(128)S(1)} %dynamic-update-slice), channel_id=1, replica_groups=mesh['seq'=32,'tensor'=8] {'seq'}, use_global_device_ids=true, to_apply=%add | all-reduce | flops 32 | bytes 256
  37.4 113.8 %all-gather.2.cloned.1.call-done = bf16[32768,256]{0,1:T(8,128)(2,1)} async-done(((bf16[1024,256]{0,1:T(8,128)(2,1)}), bf16[32768,256]{0,1:T(8,128)(2,1)}) %all-gather.2.cloned.1.call-update) | async-done | bytes 16777232 | tf_op jit(solution)/shard_map/all_gather | solution.py:64
  151.2 18.7 %copy.106 = bf16[32,8,32,1024]{3,2,1,0:T(8,128)(2,1)} copy(bf16[32,8,32,1024]{3,1,2,0:T(8,128)(2,1)} %bitcast.110) | data formatting | bytes 33554432
  169.8 23.0 %copy.79 = bf16[32,1024,2,128]{3,1,2,0:T(8,128)(2,1)} copy(bf16[32,1024,2,128]{1,0,3,2:T(8,128)(2,1)} %bitcast.108) | data formatting | bytes 33554432 | tf_op jit(solution)/shard_map/while | solution.py:81
  192.9 111.5 %while.14 = (s32[]{:T(128)}, f32[128,2]{0,1:T(2,128)S(1)}, f32[128,2]{0,1:T(2,128)S(1)}, f32[128,2,128]{2,0,1:T(8,128)S(1)}, s32[32]{0:T(128)S(1)}, /*index=5*/s...) while((s32[]{:T(128)}, f32[128,2]{0,1:T(2,128)S(1)}, ...), condition=%wide.region_7.8_spmd, body=%wide.region_1.7_spmd.sunk | while | flops 136119040 | bytes 5064039 | solution.py:81
  195.3 2.0 conditional.2
  199.8 2.1 conditional.2
  204.9 1.3 fusion.45
  209.2 2.0 conditional.2
  213.7 2.1 conditional.2
  218.9 1.3 fusion.45
  221.3 1.3 fusion.45
  223.2 2.0 conditional.2
  225.8 1.3 fusion.45
  232.6 2.0 conditional.2
  237.7 1.3 fusion.45
  239.6 2.1 conditional.2
  246.5 2.0 conditional.2
  253.5 2.1 conditional.2
  256.2 1.3 fusion.45
  258.0 2.1 conditional.2
  268.1 1.3 fusion.45
  269.9 2.0 conditional.2
  272.6 1.3 fusion.45
  274.4 2.1 conditional.2
  286.3 2.0 conditional.2
  293.3 2.1 conditional.2
  297.8 2.1 conditional.2
  302.3 2.1 conditional.2
  304.8 2.6 fusion.39
  307.8 1.8 reduce-window.6
  311.1 59.8 %reduce-scatter.3.cloned.1.call-done = f32[128,256]{1,0:T(8,128)} async-done(((f32[128,2048]{1,0:T(8,128)}), f32[128,256]{1,0:T(8,128)}) %reduce-scatter.3.cloned.1.call-update) | async-done | bytes 131088 | tf_op jit(solution)/shard_map/reduce_scatter | solution.py:97
  371.9 12.9 %psum.7 = f32[128]{0:T(128)S(1)} all-reduce(f32[128]{0:T(128)S(1)} %multiply_reduce_fusion.1), channel_id=1, replica_groups=mesh['seq'=32,'tensor'=8] {'tensor'}, use_global_device_ids=true, to_apply=%region_15.16 | all-reduce | flops 128 | bytes 1024 | tf_op jit(solution)/shard_map/psum | solution.py:101
  386.8 6.7 %scatter_custom_fusion = bf16[1536,256]{1,0:T(8,128)(2,1)} fusion(s32[768]{0:T(1024)S(1)} %fusion.33, bf16[768,256]{1,0:T(8,128)(2,1)} %reshape.156, bf16[]{:T(256)} %constant.72.clone.1), kind=kCustom, calls=%fused_computation.34 | custom fusion | bytes 786944 | tf_op jit(solution)/shard_map/scatter | solution.py:119
  393.5 32.7 %all_to_all.15 = bf16[32,2,24,256]{3,2,1,0:T(8,128)(2,1)S(1)} all-to-all(bf16[32,2,24,256]{3,2,1,0:T(8,128)(2,1)} %bitcast.111), channel_id=1, replica_groups=mesh['seq'=32,'tensor'=8] {'seq'}, dimensions={0} | all-to-all | bytes 1572864 | tf_op jit(solution)/shard_map/all_to_all | solution.py:121
  426.9 74.7 %all_to_all.16 = bf16[8,32,2,24,256]{4,3,1,2,0:T(8,128)(2,1)S(1)} all-to-all(bf16[8,32,2,24,256]{4,3,1,2,0:T(8,128)(2,1)S(1)} %stack.2), channel_id=1, replica_groups=mesh['seq'=32,'tensor'=8] {'tensor'}, dimensions={0} | all-to-all | bytes 12582912 | tf_op jit(solution)/shard_map/all_to_all | solution.py:131
  501.6 9.6 %copy.92 = bf16[32,2,24,8,256]{4,3,2,0,1:T(8,128)(2,1)} copy(bf16[32,2,24,8,256]{4,2,0,1,3:T(8,128)(2,1)S(1)} %bitcast.109) | data formatting | bytes 12582912 | tf_op jit(solution)/shard_map/reshape | solution.py:130
  511.2 10.5 %reshape.169 = bf16[32,2,24,2048,1]{3,2,0,1,4:T(8,128)(2,1)} reshape(bf16[32,2,24,8,256]{4,3,2,0,1:T(8,128)(2,1)} %copy.92) | data formatting | bytes 12582912 | tf_op jit(solution)/shard_map/reshape | solution.py:130
  521.7 5.7 fusion.9
  527.4 4.6 convert_bitcast_fusion
  532.0 39.7 %reduce-scatter.5.cloned.1.call-done = bf16[32,2,24,256]{3,2,0,1:T(8,128)(2,1)} async-done(((bf16[32,2,24,2048]{3,2,0,1:T(8,128)(2,1)}), bf16[32,2,24,256]{3,2,0,1:T(8,128)(2,1)}) %reduce-scatter.5.cloned.1.call-update) | async-done | bytes 786448 | tf_op jit(solution)/shard_map/reduce_scatter | solution.py:140
  571.6 2.1 copy.94
  573.7 10.2 %all-to-all-start.2 = ((bf16[32,2,24,256]{3,2,1,0:T(8,128)(2,1)}), bf16[32,2,24,256]{3,2,1,0:T(8,128)(2,1)}, u32[]{:S(2)}, u32[]{:S(2)}) async-start(bf16[32,2,24,256]{3,2,1,0:T(8,128)(2,1)} %copy.94), calls=%async_computation.4 | async-start | bytes 1572864 | tf_op jit(solution)/shard_map/all_to_all | solution.py:143
  584.0 22.6 %all-to-all-done.2 = bf16[32,2,24,256]{3,2,1,0:T(8,128)(2,1)} async-done(((bf16[32,2,24,256]{3,2,1,0:T(8,128)(2,1)}), bf16[32,2,24,256]{3,2,1,0:T(8,128)(2,1)}, u32[]{:S(2)}, u32[]{:S(2)}) %all-to-all-start.2) | async-done | bytes 786464 | tf_op jit(solution)/shard_map/all_to_all | solution.py:143
  606.6 3.4 gather_fusion
  611.0 1.6 multiply_reduce_fusion
  612.7 1.5 add_convert_fusion
  (247 shorter events, 93.7 us)
Async XLA Ops:
  7.2 514.5 %copy-start = (bf16[2,2048,2,176]{1,3,2,0:T(8,128)(2,1)S(1)}, bf16[2,2048,2,176]{1,3,2,0:T(8,128)(2,1)}, u32[]{:S(2)}) copy-start(bf16[2,2048,2,176]{1,3,2,0:T(8,128)(2,1)} %param.28) | copy-start | bytes 8650756
  7.2 5.5 copy-start.7
  7.2 29.8 %copy-start.4 = (s32[1,128]{1,0:T(1,128)S(1)}, s32[1,128]{1,0:T(1,128)}, u32[]{:S(2)}) copy-start(s32[1,128]{1,0:T(1,128)} %param.19) | copy-start | bytes 1540
  7.2 29.8 %copy-start.6 = (s32[1,4]{1,0:T(1,128)S(1)}, s32[1,4]{1,0:T(1,128)}, u32[]{:S(2)}) copy-start(s32[1,4]{1,0:T(1,128)} %param.20) | copy-start | bytes 52
  7.2 144.0 %all-gather.2.cloned.1.call-start = ((), (), s32[]{:S(2)}) async-start(), calls=%async_computation.5 | async-start | bytes 17301504 | tf_op jit(solution)/shard_map/all_gather | solution.py:64
  10.0 360.9 %reduce-scatter.3.cloned.1.call-start = ((), (), s32[]{:S(2)}) async-start(), calls=%async_computation.6 | async-start | bytes 1179648 | tf_op jit(solution)/shard_map/reduce_scatter | solution.py:97
  304.4 3.0 copy-start.2
  307.4 264.3 %reduce-scatter.5.cloned.1.call-start = ((), (), s32[]{:S(2)}) async-start(), calls=%async_computation.7 | async-start | bytes 7077888 | tf_op jit(solution)/shard_map/reduce_scatter | solution.py:140
  521.7 5.7 copy-start.5
  531.9 51.9 %copy-start.3 = (f32[128,6]{0,1:T(8,128)S(1)}, f32[128,6]{0,1:T(8,128)}, u32[]{:S(2)}) copy-start(f32[128,6]{0,1:T(8,128)} %param.27) | copy-start | bytes 9220
  573.7 32.9 %all-to-all-start.2 = ((bf16[32,2,24,256]{3,2,1,0:T(8,128)(2,1)}), bf16[32,2,24,256]{3,2,1,0:T(8,128)(2,1)}, u32[]{:S(2)}, u32[]{:S(2)}) async-start(bf16[32,2,24,256]{3,2,1,0:T(8,128)(2,1)} %copy.94), calls=%async_computation.4 | async-start | bytes 1572864 | tf_op jit(solution)/shard_map/all_to_all | solution.py:143
  606.6 6.1 copy-start.1
Sparse Core Ops, SparseCore 0:
  10.6 140.5 all-gather.1
  307.5 63.3 reduce-scatter.2
  532.1 39.5 reduce-scatter.4
